TPU v7x, 128 devices: a whole 4x4x4 slice. The times are simulated.
128 devices in a mesh: group: 4 (over x), expert: 32 (over y, z, core).
Axes of the slice: x: 4, y: 4, z: 4, core: 2. Of those that a mesh axis runs over, the one named last changes fastest.
Arguments:
- tokens: bfloat16 [16384, 2048], P(('group', 'expert')), may hold values from -6 to 6
- cotangent: bfloat16 [16384, 2048], P(('group', 'expert')), may hold values from -6 to 6
- gate_probs: float32 [16384, 8], P(('group', 'expert')), may hold values from 0.02 to 0.5
- expert_ids: int32 [16384, 8], P(('group', 'expert')), may hold values from 0 to 31, all different within a row; in each aligned block of 128 rows (0 to 127, 128 to 255, ...) at most 72 rows name the same one
- gate_up: bfloat16 [32, 2048, 768], P('expert'), may hold values from -0.125 to 0.125
- down_weight: bfloat16 [32, 384, 2048], P('expert'), may hold values from -0.3125 to 0.3125
- gate_up_moment: float32 [32, 2048, 768], P('expert', 'group'), may hold values from -6 to 6
- gate_up_second: float32 [32, 2048, 768], P('expert', 'group'), may hold values from 0.05 to 20
- down_moment: float32 [32, 384, 2048], P('expert', None, 'group'), may hold values from -6 to 6
- down_second: float32 [32, 384, 2048], P('expert', None, 'group'), may hold values from 0.05 to 20
Outputs:
- token_grad: bfloat16 [16384, 2048], P(('group', 'expert'))
- updated_gate_up: bfloat16 [32, 2048, 768], P('expert')
- updated_down: bfloat16 [32, 384, 2048], P('expert')
- gate_up_moment_out: float32 [32, 2048, 768], P('expert', 'group')
- gate_up_second_out: float32 [32, 2048, 768], P('expert', 'group')
- down_moment_out: float32 [32, 384, 2048], P('expert', None, 'group')
- down_second_out: float32 [32, 384, 2048], P('expert', None, 'group')
Inputs may be any that keep to these rules, and one draw needn't show every extreme that they name: `expert_ids`: each row names 8 different experts. In the rows of one device no expert is named by more than 72 rows, and in every draw some expert is named by exactly 72 rows of some device.
All inputs are finite; a program needn't handle non-finite values.
Results may differ from a plain program's by a relative error of at most 0.015.
Values may be sent and summed in bfloat16 or wider, within the bound.
No kernel may reach another device: no remote copies, remote signals or barrier semaphores. Data moves between devices by JAX's collectives and lax.ppermute only.
A program may use at most 192 MiB of HBM per device.

v0:
```python
import jax
import jax.numpy as jnp
from jax import lax
from jax.sharding import PartitionSpec as P

learn_rate = 0.001
beta_first = 0.9
beta_second = 0.999
adam_eps = 1e-08


def expert_backward(inputs, scaled_grad, weight_gate_up, weight_down):
    hidden_count = weight_down.shape[0]
    projected = jnp.dot(inputs, weight_gate_up, preferred_element_type=jnp.float32)
    gate_part = projected[:, :hidden_count]
    up_part = projected[:, hidden_count:]
    sigmoid_gate = jax.nn.sigmoid(gate_part)
    activated = gate_part * sigmoid_gate
    hidden_act = (activated * up_part).astype(jnp.bfloat16)
    hidden_grad = jnp.dot(scaled_grad, weight_down.T, preferred_element_type=jnp.float32)
    slope = sigmoid_gate * (1.0 + gate_part * (1.0 - sigmoid_gate))
    pair_grad = jnp.concatenate(
        [hidden_grad * up_part * slope, hidden_grad * activated], axis=1
    ).astype(jnp.bfloat16)
    down_grad = jnp.dot(hidden_act.T, scaled_grad, preferred_element_type=jnp.float32)
    gate_up_grad = jnp.dot(inputs.T, pair_grad, preferred_element_type=jnp.float32)
    input_grad = jnp.dot(pair_grad, weight_gate_up.T, preferred_element_type=jnp.float32).astype(
        jnp.bfloat16
    )
    return (gate_up_grad, down_grad, input_grad)


def adam_update(weight, grad, first, second):
    first_new = beta_first * first + (1.0 - beta_first) * grad
    second_new = beta_second * second + (1.0 - beta_second) * grad * grad
    updated = (
        weight.astype(jnp.float32) - learn_rate * first_new / (jnp.sqrt(second_new) + adam_eps)
    ).astype(jnp.bfloat16)
    return (updated, first_new, second_new)


def slot_layout(expert_ids, expert_count, capacity):
    flat_ids = expert_ids.reshape(-1)
    onehot = (flat_ids[:, None] == jnp.arange(expert_count, dtype=jnp.int32)[None, :]).astype(
        jnp.int32
    )
    before = jnp.cumsum(onehot, axis=0) - onehot
    slot_rank = jnp.sum(before * onehot, axis=1)
    return flat_ids * capacity + slot_rank


def local(
    tokens,
    cotangent,
    gate_probs,
    expert_ids,
    gate_up,
    down_weight,
    gate_up_moment,
    gate_up_second,
    down_moment,
    down_second,
):
    expert_count = lax.axis_size("expert")
    local_tokens, model_width = tokens.shape
    top_count = expert_ids.shape[1]
    capacity = min(local_tokens, 9 * local_tokens * top_count // (4 * expert_count))
    slot_total = expert_count * capacity
    slot_index = slot_layout(expert_ids, expert_count, capacity)
    scaled = (gate_probs[:, :, None] * cotangent.astype(jnp.float32)[:, None, :]).astype(
        jnp.bfloat16
    )
    repeated = jnp.broadcast_to(tokens[:, None, :], (local_tokens, top_count, model_width))
    payload = jnp.stack([repeated, scaled], axis=2).reshape(
        local_tokens * top_count, 2, model_width
    )
    outgoing = jnp.zeros((slot_total, 2, model_width), jnp.bfloat16).at[slot_index].set(payload)
    outgoing = outgoing.reshape(expert_count, capacity, 2, model_width)
    received = lax.all_to_all(outgoing, "expert", split_axis=0, concat_axis=0, tiled=True)
    slot_rows = received.reshape(slot_total, 2, model_width)
    weight_pair = gate_up[0]
    weight_down = down_weight[0]
    grad_pair, grad_down, row_grads = expert_backward(
        slot_rows[:, 0], slot_rows[:, 1], weight_pair, weight_down
    )
    returned = lax.all_to_all(
        row_grads.reshape(expert_count, capacity, model_width),
        "expert",
        split_axis=0,
        concat_axis=0,
        tiled=True,
    )
    returned = returned.reshape(slot_total, model_width)
    token_grad = jnp.sum(
        returned[slot_index].reshape(local_tokens, top_count, model_width).astype(jnp.float32),
        axis=1,
    ).astype(jnp.bfloat16)
    sum_pair, sum_down = (
        lax.psum_scatter(
            grad_pair[None].astype(jnp.bfloat16), "group", scatter_dimension=1, tiled=True
        ).astype(jnp.float32),
        lax.psum_scatter(
            grad_down[None].astype(jnp.bfloat16), "group", scatter_dimension=2, tiled=True
        ).astype(jnp.float32),
    )
    group_index = lax.axis_index("group")
    share_rows = model_width // lax.axis_size("group")
    own_pair = lax.dynamic_slice_in_dim(gate_up, group_index * share_rows, share_rows, 1)
    own_down = lax.dynamic_slice_in_dim(down_weight, group_index * share_rows, share_rows, 2)
    new_pair, first_pair, second_pair = adam_update(
        own_pair, sum_pair, gate_up_moment, gate_up_second
    )
    new_down, first_down, second_down = adam_update(own_down, sum_down, down_moment, down_second)
    full_pair, full_down = (
        lax.all_gather(new_pair, "group", axis=1, tiled=True),
        lax.all_gather(new_down, "group", axis=2, tiled=True),
    )
    return (token_grad, full_pair, full_down, first_pair, second_pair, first_down, second_down)


def solution(mesh):
    placed = (
        P(("group", "expert"), None),
        P(("group", "expert"), None),
        P(("group", "expert"), None),
        P(("group", "expert"), None),
        P("expert", None, None),
        P("expert", None, None),
        P("expert", "group", None),
        P("expert", "group", None),
        P("expert", None, "group"),
        P("expert", None, "group"),
    )
    return jax.shard_map(
        local,
        mesh=mesh,
        in_specs=placed,
        out_specs=(
            P(("group", "expert"), None),
            P("expert", None, None),
            P("expert", None, None),
            P("expert", "group", None),
            P("expert", "group", None),
            P("expert", None, "group"),
            P("expert", None, "group"),
        ),
        check_vma=False,
    )
```

profile of v0, /device:TPU:48, one launch (start us, length us, event | category | flops | bytes accessed | tf_op | source)
XLA Modules:
  0.0 650.9 jit_solution(8910196216144405654)
XLA Ops:
  7.2 0.0 reduce-scatter.5.cloned.1.call-start
  7.2 0.7 broadcast_multiply_fusion
  8.0 0.8 copy.24
  8.8 0.1 eq.29
  8.8 0.1 eq.25
  8.9 0.1 copy.23
  9.0 0.1 mul.125
  9.1 0.8 copy.28
  9.9 0.1 mul.127
  10.0 9.0 %reduce-window.6 = s32[32,8,128]{2,1,0:T(8,128)S(1)} reduce-window(s32[32,8,128]{2,1,0:T(8,128)S(1)} %fusion.21, s32[]{:T(128)} %constant.16.clone.1), window={size=1x1x128 pad=0_0x0_0x127_0}, to_apply=%region_0.0 | reduce-window | flops 4161536 | bytes 262148 | tf_op jit(solution)/shard_map/reduce-window
  19.1 0.1 slice.26
  19.2 0.1 copy.26
  19.3 0.1 copy.27
  19.4 0.1 broadcast_add_fusion
  19.5 1.1 convert_element_type.62
  20.7 0.7 broadcast_bitcast_fusion
  21.3 2.4 fusion
  23.8 6.2 pad_maximum_fusion
  29.9 16.4 %copy.29 = bf16[1024,2,2048]{2,1,0:T(2,128)(2,1)} copy(bf16[1024,2,2048]{2,0,1:T(8,128)(2,1)} %pad_maximum_fusion) | data formatting | bytes 16777216 | tf_op jit(solution)/shard_map/stack | solution.py:74
  46.4 11.2 %broadcast_in_dim.2 = bf16[2304,2,2048]{2,1,0:T(2,128)(2,1)} broadcast(bf16[]{:T(256)} %constant.14.clone.1), dimensions={} | broadcast | bytes 18874370 | tf_op jit(solution)/shard_map/broadcast_in_dim | solution.py:77
  57.6 128.4 %scatter_fusion = bf16[2304,2,2048]{2,1,0:T(2,128)(2,1)} fusion(bf16[2304,2,2048]{2,1,0:T(2,128)(2,1)} %broadcast_in_dim.2, s32[1024]{0:T(1024)S(1)} %bitcast.72, bf16[1024,2,2048]{2,1,0:T(2,128)(2,1)} %copy.29), kind=kCustom, calls=%fused_computation.1 | custom fusion | bytes 25169920 | tf_op jit(solution)/shard_map/scatter | solution.py:77
  186.0 212.7 %all_to_all.10 = bf16[32,72,2,2048]{3,2,1,0:T(2,128)(2,1)S(1)} all-to-all(bf16[32,72,2,2048]{3,2,1,0:T(2,128)(2,1)} %bitcast.65), channel_id=1, replica_groups=mesh['group'=4,'expert'=32] {'expert'}, dimensions={0} | all-to-all | bytes 37748736 | tf_op jit(solution)/shard_map/all_to_all | solution.py:79
  398.7 9.5 %copy.30 = bf16[32,72,2,2048]{3,1,0,2:T(8,128)(2,1)} copy(bf16[32,72,2,2048]{3,2,1,0:T(2,128)(2,1)S(1)} %all_to_all.10) | data formatting | bytes 37748736 | tf_op jit(solution)/shard_map/all_to_all | solution.py:79
  408.2 10.0 %fusion.4 = f32[2304,768]{0,1:T(8,128)S(1)} fusion(bf16[2304,2,2048]{2,0,1:T(8,128)(2,1)} %bitcast.66, bf16[1,2048,768]{2,1,0:T(8,128)(2,1)S(1)} %copy-done.5), kind=kOutput, calls=%fused_computation.11 | convolution fusion | flops 7247757312 | bytes 19660800 | tf_op jit(solution)/shard_map/dot_general | solution.py:14
  418.2 2.9 copy-done.7
  421.1 8.8 %fusion.11 = bf16[1,384,2048]{2,1,0:T(8,128)(2,1)} fusion(bf16[2304,2,2048]{2,0,1:T(8,128)(2,1)} %bitcast.67, f32[2304,768]{0,1:T(8,128)S(1)} %fusion.4), kind=kOutput, calls=%fused_computation.24 | convolution fusion | flops 3629973504 | bytes 18087936 | tf_op jit(solution)/shard_map/dot_general | solution.py:25
  430.0 0.0 reduce-scatter.5.cloned.1.call-update
  430.0 0.2 reduce-scatter.3.cloned.1.call-start
  430.2 8.6 %multiply_convert_fusion.2 = (bf16[2304,384]{0,1:T(8,128)(2,1)S(1)}, bf16[2304,384]{0,1:T(8,128)(2,1)S(1)}) fusion(f32[2304,768]{0,1:T(8,128)} %copy-done.7, bf16[1,384,2048]{2,1,0:T(8,128)(2,1)S(1)} %copy-done.6, bf16[2304,2,2048]{2,0,1:T(8,128)(2,1)} %bitcast.68), kind=kOutput, calls=%fused_computation.16 | convolution fusion | flops 3635380224 | bytes 21626880 | tf_op jit(solution)/shard_map/dot_general | solution.py:20
  438.8 1.2 copy-done.8
  440.0 0.6 copy-done.9
  440.6 11.3 %fusion.9 = bf16[1,2048,768]{2,1,0:T(8,128)(2,1)} fusion(bf16[2304,2,2048]{2,0,1:T(8,128)(2,1)} %bitcast.69, bf16[2304,384]{0,1:T(8,128)(2,1)S(1)} %get-tuple-element.14, bf16[2304,384]{0,1:T(8,128)(2,1)S(1)} %get-tuple-element.13), kind=kOutput, calls=%fused_computation.22 | convolution fusion | flops 7256408064 | bytes 16121856 | tf_op jit(solution)/shard_map/dot_general | solution.py:26
  451.9 0.0 reduce-scatter.3.cloned.1.call-update
  451.9 12.6 %convolution_convert_fusion = bf16[2304,2048]{1,0:T(8,128)(2,1)} fusion(bf16[1,2048,768]{2,1,0:T(8,128)(2,1)} %param.14, bf16[2304,384]{0,1:T(8,128)(2,1)} %copy-done.9, bf16[2304,384]{0,1:T(8,128)(2,1)} %copy-done.8), kind=kOutput, calls=%fused_computation.2 | convolution fusion | flops 7259553792 | bytes 16121856 | tf_op jit(solution)/shard_map/dot_general | solution.py:27
  464.5 8.2 %all-to-all-start.1 = ((bf16[32,72,2048]{2,1,0:T(8,128)(2,1)}), bf16[32,72,2048]{2,1,0:T(8,128)(2,1)}, u32[]{:S(2)}, u32[]{:S(2)}) async-start(bf16[32,72,2048]{2,1,0:T(8,128)(2,1)} %bitcast.70), calls=%async_computation.1 | async-start | bytes 18874368 | tf_op jit(solution)/shard_map/all_to_all | solution.py:86
  472.7 0.0 all-gather.5.cloned.1.call-start
  472.8 0.0 reduce-scatter.5.cloned.1.call-done
  472.8 3.1 subtract_convert_fusion.1
  475.9 0.0 all-gather.5.cloned.1.call-update
  475.9 0.3 all-gather.3.cloned.1.call-start
  476.2 21.6 %reduce-scatter.3.cloned.1.call-done = bf16[1,512,768]{2,1,0:T(8,128)(2,1)} async-done(((bf16[1,2048,768]{2,1,0:T(8,128)(2,1)}), bf16[1,512,768]{2,1,0:T(8,128)(2,1)}) %reduce-scatter.3.cloned.1.call-update) | async-done | bytes 786448 | tf_op jit(solution)/shard_map/reduce_scatter | solution.py:99
  497.8 4.4 subtract_convert_fusion
  502.2 24.1 %all-gather.5.cloned.1.call-done = bf16[1,384,2048]{2,1,0:T(8,128)(2,1)} async-done(((bf16[1,384,512]{2,1,0:T(8,128)(2,1)}), bf16[1,384,2048]{2,1,0:T(8,128)(2,1)}) %all-gather.5.cloned.1.call-update) | async-done | bytes 1572880 | tf_op jit(solution)/shard_map/all_gather | solution.py:116
  526.3 93.4 %all-to-all-done.1 = bf16[32,72,2048]{2,1,0:T(8,128)(2,1)} async-done(((bf16[32,72,2048]{2,1,0:T(8,128)(2,1)}), bf16[32,72,2048]{2,1,0:T(8,128)(2,1)}, u32[]{:S(2)}, u32[]{:S(2)}) %all-to-all-start.1) | async-done | bytes 9437216 | tf_op jit(solution)/shard_map/all_to_all | solution.py:86
  619.7 13.7 %gather_fusion = bf16[1024,2048]{1,0:T(8,128)(2,1)} fusion(bf16[2304,2048]{1,0:T(8,128)(2,1)} %bitcast.13, s32[1024]{0:T(1024)S(1)} %broadcast_clamp_fusion), kind=kCustom, calls=%fused_computation | custom fusion | bytes 8392704 | tf_op jit(solution)/shard_map/gather | solution.py:95
  633.4 5.9 bitcast_reduce_fusion
  639.3 3.9 copy.36
  643.2 1.1 copy.37
  (25 shorter events, 0.2 us)
Async XLA Ops:
  7.2 13.5 %copy-start = (bf16[128,2048]{1,0:T(8,128)(2,1)S(1)}, bf16[128,2048]{1,0:T(8,128)(2,1)}, u32[]{:S(2)}) copy-start(bf16[128,2048]{1,0:T(8,128)(2,1)} %param.10) | copy-start | bytes 1572868
  7.2 465.6 %reduce-scatter.5.cloned.1.call-start = ((), (), s32[]{:S(2)}) async-start(), calls=%async_computation.6 | async-start | bytes 1966080 | tf_op jit(solution)/shard_map/reduce_scatter | solution.py:102
  398.7 9.5 %copy-start.5 = (bf16[1,2048,768]{2,1,0:T(8,128)(2,1)S(1)}, bf16[1,2048,768]{2,1,0:T(8,128)(2,1)}, u32[]{:S(2)}) copy-start(bf16[1,2048,768]{2,1,0:T(8,128)(2,1)} %param.14) | copy-start | bytes 9437188
  418.2 2.9 copy-start.7
  421.1 9.1 %copy-start.6 = (bf16[1,384,2048]{2,1,0:T(8,128)(2,1)S(1)}, bf16[1,384,2048]{2,1,0:T(8,128)(2,1)}, u32[]{:S(2)}) copy-start(bf16[1,384,2048]{2,1,0:T(8,128)(2,1)} %param.15) | copy-start | bytes 4718596
  430.0 67.8 %reduce-scatter.3.cloned.1.call-start = ((), (), s32[]{:S(2)}) async-start(), calls=%async_computation.4 | async-start | bytes 3932160 | tf_op jit(solution)/shard_map/reduce_scatter | solution.py:99
  438.8 1.2 copy-start.8
  438.8 1.8 copy-start.9
  464.5 8.3 %copy-start.4 = (f32[1,384,512]{2,1,0:T(8,128)S(1)}, f32[1,384,512]{2,1,0:T(8,128)}, u32[]{:S(2)}) copy-start(f32[1,384,512]{2,1,0:T(8,128)} %param.18) | copy-start | bytes 2359300
  464.5 155.2 %all-to-all-start.1 = ((bf16[32,72,2048]{2,1,0:T(8,128)(2,1)}), bf16[32,72,2048]{2,1,0:T(8,128)(2,1)}, u32[]{:S(2)}, u32[]{:S(2)}) async-start(bf16[32,72,2048]{2,1,0:T(8,128)(2,1)} %bitcast.70), calls=%async_computation.1 | async-start | bytes 18874368 | tf_op jit(solution)/shard_map/all_to_all | solution.py:86
  472.7 25.0 %copy-start.3 = (f32[1,512,768]{2,1,0:T(8,128)S(1)}, f32[1,512,768]{2,1,0:T(8,128)}, u32[]{:S(2)}) copy-start(f32[1,512,768]{2,1,0:T(8,128)} %param.16) | copy-start | bytes 4718596
  472.7 53.5 %all-gather.5.cloned.1.call-start = ((), (), s32[]{:S(2)}) async-start(), calls=%async_computation.7 | async-start | bytes 1966080 | tf_op jit(solution)/shard_map/all_gather | solution.py:116
  475.9 163.4 %all-gather.3.cloned.1.call-start = ((), (), s32[]{:S(2)}) async-start(), calls=%async_computation.5 | async-start | bytes 3932160 | tf_op jit(solution)/shard_map/all_gather | solution.py:115
  639.3 3.9 copy-start.2
  639.3 5.1 copy-start.1
Sparse Core Ops, SparseCore 0:
  430.1 26.6 reduce-scatter.4
  459.8 37.9 reduce-scatter.2
  500.0 26.2 all-gather.4
  528.4 39.5 all-gather.2
where the time goes:
time: 653 us; the launch traced here: 651 us
  blocking collectives  213 us (33%)
  local copies, waits for them, and re-layouts  192 us (29%)
  waiting for transfers between devices  139 us (21%)
  matrix products  51.3 us (8%)
  other arithmetic  33.1 us (5%)
  between operations  14 us (2%)
  starting transfers between devices  8.73 us (1%)
    all_to_all x1, blocking collectives, local(): lax.all_to_all(outgoing, 'expert', split_axis=0, concat_axis=0, tiled=True)  213 us
    scatter x1, local copies, waits for them, and re-layouts, local(): jnp.zeros((slot_total, 2, model_width), jnp.bfloat16).at[slot_index]  128 us
    all_to_all x1, waiting for transfers between devices, local(): lax.all_to_all(row_grads.reshape(expert_count, capacity, model_width), 'e...  93.4 us
    all_gather x1, waiting for transfers between devices, local(): lax.all_gather(new_down, 'group', axis=2, tiled=True)  24.1 us
    reduce_scatter x1, waiting for transfers between devices, local(): lax.psum_scatter(grad_pair[None].astype(jnp.bfloat16), 'group', scatter_d...  21.6 us
    another operation x2, local copies, waits for them, and re-layouts, local(): jnp.stack([repeated, scaled], axis=2)  17 us
    gather x1, local copies, waits for them, and re-layouts, local(): returned[slot_index].reshape(local_tokens, top_count, model_width)  13.7 us
  transfers between devices with their start and end apart: 5, of which 3 were waited for; matrix products, arithmetic and copies ran while one was open for 9% of the time, Pallas kernels for 0%

commit v1 on v0

--- a/solution.py
+++ b/solution.py
@@ -113,7 +113,9 @@
     new_down, first_down, second_down = adam_update(own_down, sum_down, down_moment, down_second)
     full_pair, full_down = (
         lax.all_gather(new_pair, "group", axis=1, tiled=True),
-        lax.all_gather(new_down, "group", axis=2, tiled=True),
+        jnp.concatenate(
+            lax.all_to_all(jnp.stack([new_down] * lax.axis_size("group")), "group", 0, 0), axis=2
+        ),
     )
     return (token_grad, full_pair, full_down, first_pair, second_pair, first_down, second_down)
 

time: 653 us -> 684 us (1.047)
  waiting for transfers between devices: 139 us -> 163 us
    all_to_all x1, waiting for transfers between devices: 93.4 us -> 132 us  [local(): lax.all_to_all(row_grads.reshape(expert_count, capacity, model_width), 'e...]
    all_gather x1 -> x0, waiting for transfers between devices: 24.1 us -> none  [local(): lax.all_gather(new_down, 'group', axis=2, tiled=True)]
    all_to_all x0 -> x1, waiting for transfers between devices: none -> 22.2 us  [local(): lax.all_to_all(jnp.stack([new_down] * lax.axis_size('group')), 'group', 0...]
    reduce_scatter x1, waiting for transfers between devices: 21.6 us -> 3.53 us  [local(): lax.psum_scatter(grad_pair[None].astype(jnp.bfloat16), 'group', scatter_d...]
  transfers between devices with their start and end apart: 5 -> 5, of which waited for: 3 -> 4; matrix products, arithmetic and copies ran while one was open for 9% -> 10% of each run, Pallas kernels for 0% -> 0%
where the time goes in v1:
time: 684 us; the launch traced here: 682 us
  blocking collectives  213 us (31%)
  local copies, waits for them, and re-layouts  196 us (29%)
  waiting for transfers between devices  163 us (24%)
  matrix products  51.3 us (8%)
  other arithmetic  33.3 us (5%)
  between operations  13.9 us (2%)
  starting transfers between devices  11.6 us (2%)
    all_to_all x1, blocking collectives, local(): lax.all_to_all(outgoing, 'expert', split_axis=0, concat_axis=0, tiled=True)  213 us
    all_to_all x1, waiting for transfers between devices, local(): lax.all_to_all(row_grads.reshape(expert_count, capacity, model_width), 'e...  132 us
    scatter x1, local copies, waits for them, and re-layouts, local(): jnp.zeros((slot_total, 2, model_width), jnp.bfloat16).at[slot_index]  128 us
    all_to_all x1, waiting for transfers between devices, local(): lax.all_to_all(jnp.stack([new_down] * lax.axis_size('group')), 'group', 0...  22.2 us
    another operation x2, local copies, waits for them, and re-layouts, local(): jnp.stack([repeated, scaled], axis=2)  17 us
    gather x1, local copies, waits for them, and re-layouts, local(): returned[slot_index].reshape(local_tokens, top_count, model_width)  13.7 us
  transfers between devices with their start and end apart: 5, of which 4 were waited for; matrix products, arithmetic and copies ran while one was open for 10% of the time, Pallas kernels for 0%

profile of v1, /device:TPU:48, one launch (start us, length us, event | category | flops | bytes accessed | tf_op | source)
XLA Modules:
  0.0 681.9 jit_solution(10199177369274549076)
XLA Ops:
  7.2 0.0 reduce-scatter.5.cloned.1.call-start
  7.2 0.7 broadcast_multiply_fusion
  8.0 0.8 copy.40
  8.8 0.1 eq.29
  8.8 0.1 eq.25
  8.9 0.1 copy.39
  9.0 0.1 mul.125
  9.1 0.8 copy.44
  9.9 0.1 mul.127
  10.0 9.0 %reduce-window.6 = s32[32,8,128]{2,1,0:T(8,128)S(1)} reduce-window(s32[32,8,128]{2,1,0:T(8,128)S(1)} %fusion.22, s32[]{:T(128)} %constant.16.clone.1), window={size=1x1x128 pad=0_0x0_0x127_0}, to_apply=%region_0.0 | reduce-window | flops 4161536 | bytes 262148 | tf_op jit(solution)/shard_map/reduce-window
  19.1 0.1 slice.26
  19.2 0.1 copy.42
  19.3 0.1 copy.43
  19.4 0.1 broadcast_add_fusion
  19.5 1.1 convert_element_type.64
  20.7 0.7 broadcast_bitcast_fusion
  21.3 2.4 fusion
  23.7 6.2 pad_maximum_fusion
  29.9 16.4 %copy.45 = bf16[1024,2,2048]{2,1,0:T(2,128)(2,1)} copy(bf16[1024,2,2048]{2,0,1:T(8,128)(2,1)} %pad_maximum_fusion) | data formatting | bytes 16777216 | tf_op jit(solution)/shard_map/stack | solution.py:74
  46.3 11.2 %broadcast_in_dim.2 = bf16[2304,2,2048]{2,1,0:T(2,128)(2,1)} broadcast(bf16[]{:T(256)} %constant.14.clone.1), dimensions={} | broadcast | bytes 18874370 | tf_op jit(solution)/shard_map/broadcast_in_dim | solution.py:77
  57.5 128.4 %scatter_fusion = bf16[2304,2,2048]{2,1,0:T(2,128)(2,1)} fusion(bf16[2304,2,2048]{2,1,0:T(2,128)(2,1)} %broadcast_in_dim.2, s32[1024]{0:T(1024)S(1)} %bitcast.78, bf16[1024,2,2048]{2,1,0:T(2,128)(2,1)} %copy.45), kind=kCustom, calls=%fused_computation.1 | custom fusion | bytes 25169920 | tf_op jit(solution)/shard_map/scatter | solution.py:77
  186.0 212.7 %all_to_all.15 = bf16[32,72,2,2048]{3,2,1,0:T(2,128)(2,1)S(1)} all-to-all(bf16[32,72,2,2048]{3,2,1,0:T(2,128)(2,1)} %bitcast.70), channel_id=1, replica_groups=mesh['group'=4,'expert'=32] {'expert'}, dimensions={0} | all-to-all | bytes 37748736 | tf_op jit(solution)/shard_map/all_to_all | solution.py:79
  398.6 9.5 %copy.46 = bf16[32,72,2,2048]{3,1,0,2:T(8,128)(2,1)} copy(bf16[32,72,2,2048]{3,2,1,0:T(2,128)(2,1)S(1)} %all_to_all.15) | data formatting | bytes 37748736 | tf_op jit(solution)/shard_map/all_to_all | solution.py:79
  408.2 10.0 %fusion.4 = f32[2304,768]{0,1:T(8,128)S(1)} fusion(bf16[2304,2,2048]{2,0,1:T(8,128)(2,1)} %bitcast.71, bf16[1,2048,768]{2,1,0:T(8,128)(2,1)S(1)} %copy-done.4), kind=kOutput, calls=%fused_computation.11 | convolution fusion | flops 7247757312 | bytes 19660800 | tf_op jit(solution)/shard_map/dot_general | solution.py:14
  418.2 2.9 copy-done.6
  421.1 8.8 %fusion.11 = bf16[1,384,2048]{2,1,0:T(8,128)(2,1)} fusion(bf16[2304,2,2048]{2,0,1:T(8,128)(2,1)} %bitcast.72, f32[2304,768]{0,1:T(8,128)S(1)} %fusion.4), kind=kOutput, calls=%fused_computation.24 | convolution fusion | flops 3629973504 | bytes 18087936 | tf_op jit(solution)/shard_map/dot_general | solution.py:25
  429.9 0.0 reduce-scatter.5.cloned.1.call-update
  430.0 0.2 reduce-scatter.3.cloned.1.call-start
  430.2 8.6 %multiply_convert_fusion.2 = (bf16[2304,384]{0,1:T(8,128)(2,1)S(1)}, bf16[2304,384]{0,1:T(8,128)(2,1)S(1)}) fusion(f32[2304,768]{0,1:T(8,128)} %copy-done.6, bf16[1,384,2048]{2,1,0:T(8,128)(2,1)S(1)} %copy-done.5, bf16[2304,2,2048]{2,0,1:T(8,128)(2,1)} %bitcast.73), kind=kOutput, calls=%fused_computation.16 | convolution fusion | flops 3635380224 | bytes 21626880 | tf_op jit(solution)/shard_map/dot_general | solution.py:20
  438.8 1.2 copy-done.7
  440.0 0.6 copy-done.8
  440.6 11.3 %fusion.9 = bf16[1,2048,768]{2,1,0:T(8,128)(2,1)} fusion(bf16[2304,2,2048]{2,0,1:T(8,128)(2,1)} %bitcast.74, bf16[2304,384]{0,1:T(8,128)(2,1)S(1)} %get-tuple-element.21, bf16[2304,384]{0,1:T(8,128)(2,1)S(1)} %get-tuple-element.20), kind=kOutput, calls=%fused_computation.22 | convolution fusion | flops 7256408064 | bytes 16121856 | tf_op jit(solution)/shard_map/dot_general | solution.py:26
  451.9 4.9 reduce-scatter.5.cloned.1.call-done
  456.8 2.8 fusion.18
  459.6 1.3 stack.5
  460.9 3.6 all-to-all-start.2
  464.4 12.6 %convolution_convert_fusion = bf16[2304,2048]{1,0:T(8,128)(2,1)} fusion(bf16[1,2048,768]{2,1,0:T(8,128)(2,1)} %param.14, bf16[2304,384]{0,1:T(8,128)(2,1)} %copy-done.8, bf16[2304,384]{0,1:T(8,128)(2,1)} %copy-done.7), kind=kOutput, calls=%fused_computation.2 | convolution fusion | flops 7259553792 | bytes 16121856 | tf_op jit(solution)/shard_map/dot_general | solution.py:27
  477.1 22.2 %all-to-all-done.2 = bf16[4,1,384,512]{3,2,1,0:T(8,128)(2,1)S(1)} async-done(((bf16[4,1,384,512]{3,2,1,0:T(8,128)(2,1)}), bf16[4,1,384,512]{3,2,1,0:T(8,128)(2,1)S(1)}, u32[]{:S(2)}, u32[]{:S(2)}) %all-to-all-start.2) | async-done | bytes 1572896 | tf_op jit(solution)/shard_map/all_to_all | solution.py:117
  499.3 7.5 %all-to-all-start.1 = ((bf16[32,72,2048]{2,1,0:T(8,128)(2,1)}), bf16[32,72,2048]{2,1,0:T(8,128)(2,1)}, u32[]{:S(2)}, u32[]{:S(2)}) async-start(bf16[32,72,2048]{2,1,0:T(8,128)(2,1)} %bitcast.75), calls=%async_computation.1 | async-start | bytes 18874368 | tf_op jit(solution)/shard_map/all_to_all | solution.py:86
  506.8 0.3 all-gather.2.cloned.1.call-start
  507.1 3.5 reduce-scatter.3.cloned.1.call-done
  510.6 4.9 subtract_convert_fusion
  515.5 1.6 copy.47
  517.1 2.6 copy.48
  519.7 132.3 %all-to-all-done.1 = bf16[32,72,2048]{2,1,0:T(8,128)(2,1)} async-done(((bf16[32,72,2048]{2,1,0:T(8,128)(2,1)}), bf16[32,72,2048]{2,1,0:T(8,128)(2,1)}, u32[]{:S(2)}, u32[]{:S(2)}) %all-to-all-start.1) | async-done | bytes 9437216 | tf_op jit(solution)/shard_map/all_to_all | solution.py:86
  652.0 13.7 %gather_fusion = bf16[1024,2048]{1,0:T(8,128)(2,1)} fusion(bf16[2304,2048]{1,0:T(8,128)(2,1)} %bitcast.13, s32[1024]{0:T(1024)S(1)} %broadcast_clamp_fusion), kind=kCustom, calls=%fused_computation | custom fusion | bytes 8392704 | tf_op jit(solution)/shard_map/gather | solution.py:95
  665.7 5.9 bitcast_reduce_fusion
  671.7 3.8 copy.53
  (24 shorter events, 0.2 us)
Async XLA Ops:
  7.2 13.5 %copy-start = (bf16[128,2048]{1,0:T(8,128)(2,1)S(1)}, bf16[128,2048]{1,0:T(8,128)(2,1)}, u32[]{:S(2)}) copy-start(bf16[128,2048]{1,0:T(8,128)(2,1)} %param.10) | copy-start | bytes 1572868
  7.2 449.6 %reduce-scatter.5.cloned.1.call-start = ((), (), s32[]{:S(2)}) async-start(), calls=%async_computation.7 | async-start | bytes 1966080 | tf_op jit(solution)/shard_map/reduce_scatter | solution.py:102
  398.6 9.5 %copy-start.4 = (bf16[1,2048,768]{2,1,0:T(8,128)(2,1)S(1)}, bf16[1,2048,768]{2,1,0:T(8,128)(2,1)}, u32[]{:S(2)}) copy-start(bf16[1,2048,768]{2,1,0:T(8,128)(2,1)} %param.14) | copy-start | bytes 9437188
  418.2 2.9 copy-start.6
  421.1 9.1 %copy-start.5 = (bf16[1,384,2048]{2,1,0:T(8,128)(2,1)S(1)}, bf16[1,384,2048]{2,1,0:T(8,128)(2,1)}, u32[]{:S(2)}) copy-start(bf16[1,384,2048]{2,1,0:T(8,128)(2,1)} %param.15) | copy-start | bytes 4718596
  430.0 80.6 %reduce-scatter.3.cloned.1.call-start = ((), (), s32[]{:S(2)}) async-start(), calls=%async_computation.5 | async-start | bytes 3932160 | tf_op jit(solution)/shard_map/reduce_scatter | solution.py:99
  438.8 1.2 copy-start.7
  438.8 1.8 copy-start.8
  451.9 4.9 copy-start.2
  451.9 4.9 copy-start.3
  460.9 38.4 %all-to-all-start.2 = ((bf16[4,1,384,512]{3,2,1,0:T(8,128)(2,1)}), bf16[4,1,384,512]{3,2,1,0:T(8,128)(2,1)S(1)}, u32[]{:S(2)}, u32[]{:S(2)}) async-start(bf16[4,1,384,512]{3,2,1,0:T(8,128)(2,1)} %stack.5), calls=%async_computation.4 | async-start | bytes 3145728 | tf_op jit(solution)/shard_map/all_to_all | solution.py:117
  499.3 152.7 %all-to-all-start.1 = ((bf16[32,72,2048]{2,1,0:T(8,128)(2,1)}), bf16[32,72,2048]{2,1,0:T(8,128)(2,1)}, u32[]{:S(2)}, u32[]{:S(2)}) async-start(bf16[32,72,2048]{2,1,0:T(8,128)(2,1)} %bitcast.75), calls=%async_computation.1 | async-start | bytes 18874368 | tf_op jit(solution)/shard_map/all_to_all | solution.py:86
  506.8 164.9 %all-gather.2.cloned.1.call-start = ((), (), s32[]{:S(2)}) async-start(), calls=%async_computation.6 | async-start | bytes 3932160 | tf_op jit(solution)/shard_map/all_gather | solution.py:115
  665.7 9.7 %copy-start.1 = (bf16[128,2048]{1,0:T(8,128)(2,1)S(1)}, bf16[128,2048]{1,0:T(8,128)(2,1)}, u32[]{:S(2)}) copy-start(bf16[128,2048]{1,0:T(8,128)(2,1)} %param.10) | copy-start | bytes 1572868
Sparse Core Ops, SparseCore 0:
  430.1 26.6 reduce-scatter.4
  459.8 50.7 reduce-scatter.2
  515.6 39.2 all-gather.1
